TPU v7x, 32 devices: a whole 2x2x4 slice. The times are simulated.
32 devices in a mesh: mol: 2 (over x), occ: 16 (over z, y, core).
Axes of the slice: x: 2, y: 2, z: 4, core: 2. Of those that a mesh axis runs over, the one named last changes fastest.
Arguments:
- integrals: bfloat16 [512, 128, 2048], P(('mol', 'occ')), parts along dimension 0, may hold values from -6 to 6
- orbitals: bfloat16 [4096, 1536], P('mol'), parts along dimension 0
- occ_energy: float32 [256], P('mol'), parts along dimension 0, may hold values from -2 to -0.3
- vir_energy: float32 [3072], P('mol'), parts along dimension 0, may hold values from 0.1 to 3
- owner: int32 [16], P('mol'), parts along dimension 0, may hold values from 0 to 127
- vblock: int32 [16], P('mol'), parts along dimension 0, may hold values from 0 to 7
Outputs:
- factors: bfloat16 [512, 128, 1536], P('mol', 'occ'), parts along dimension 0
- pair_energy: float32 [256, 8], P(('mol', 'occ')), parts along dimension 0
There are 2 independent parts, one for each index of `mol`. A program takes and returns all parts, laid end to end along the dimension named above; each array names one. Nothing has to cross between parts.
Inputs may be any that keep to these rules, and one draw needn't show every extreme that they name: `owner`: each step names one occupied orbital and one virtual block; steps may repeat.
All inputs are finite; a program needn't handle non-finite values.
Results may differ from a plain program's by a relative error of at most 0.001.
Values may be sent and summed in bfloat16 or wider, within the bound.
No kernel may reach another device: no remote copies, remote signals or barrier semaphores. Data moves between devices by JAX's collectives and lax.ppermute only.
A program may use at most 128 MiB of HBM per device.

v0:
```python
import jax
import jax.numpy as jnp
from jax import lax
from jax.sharding import PartitionSpec as P

VBLK = 192


def pair_column(factors, block, occ_here, occ_energy, vir_energy, orbital_j, block_id):
    coulomb = lax.dot_general(
        factors, block, (((0,), (0,)), ((), ())), preferred_element_type=jnp.float32
    )
    vir_block = lax.dynamic_slice(vir_energy, (block_id * VBLK,), (VBLK,))
    occ_j = occ_energy[orbital_j]
    denom = vir_energy[None, :, None] + vir_block[None, None, :] - occ_here[:, None, None] - occ_j
    scale = 1.0 / (factors.shape[0] * vir_energy.shape[0] * VBLK)
    return -jnp.sum(coulomb * coulomb / denom, axis=(1, 2)) * scale


def per_device(integrals, orbitals, occ_energy, vir_energy, owner, vblock):
    aux_here, occ_total, basis_count = integrals.shape
    step_count = owner.shape[0]
    flat = integrals.reshape(aux_here * occ_total, basis_count)
    product = jnp.dot(flat, orbitals, preferred_element_type=jnp.float32).astype(jnp.bfloat16)
    product = product.reshape(aux_here, occ_total, orbitals.shape[1])

    def own_piece(step):
        piece = lax.dynamic_slice(
            product, (jnp.int32(0), owner[step], vblock[step] * VBLK), (aux_here, 1, VBLK)
        )
        return piece[:, 0, :]

    pieces = jnp.stack([own_piece(step) for step in range(step_count)], axis=1)
    blocks = lax.all_gather(pieces, "occ", axis=0, tiled=True)
    factors = lax.all_to_all(product, "occ", split_axis=1, concat_axis=0, tiled=True)
    local_count = factors.shape[1]
    occ_here = lax.dynamic_slice(occ_energy, (lax.axis_index("occ") * local_count,), (local_count,))
    energies = jnp.zeros((local_count, step_count), jnp.float32)

    def step_body(step, energies):
        orbital_j = owner[step]
        block_id = vblock[step]
        block = lax.dynamic_index_in_dim(blocks, step, axis=1, keepdims=False)
        column = pair_column(factors, block, occ_here, occ_energy, vir_energy, orbital_j, block_id)
        return lax.dynamic_update_slice(energies, column[:, None], (jnp.int32(0), step))

    energies = lax.fori_loop(0, step_count, step_body, energies)
    return (factors, energies)


def solution(mesh):
    placed = (P(("mol", "occ"), None, None), P("mol", None), P("mol"), P("mol"), P("mol"), P("mol"))
    return jax.shard_map(
        per_device,
        mesh=mesh,
        in_specs=placed,
        out_specs=(P("mol", "occ", None), P(("mol", "occ"), None)),
        check_vma=False,
    )
```

profile of v0, /device:TPU:9, one launch (start us, length us, event | category | flops | bytes accessed | tf_op | source)
XLA Modules:
  0.0 285.7 jit_solution(6650717841820332586)
XLA Ops:
  0.6 17.3 %convolution_convert_fusion = bf16[2048,1536]{1,0:T(8,128)(2,1)S(1)} fusion(bf16[2048,2048]{1,0:T(8,128)(2,1)} %bitcast.56, bf16[2048,1536]{1,0:T(8,128)(2,1)} %param.9), kind=kOutput, calls=%fused_computation.7 | convolution fusion | flops 12888047616 | bytes 20971520 | tf_op jit(solution)/shard_map/dot_general | solution.py:24
  17.9 2.6 copy-done.1
  20.5 6.2 %copy.19 = bf16[16,128,1536]{2,0,1:T(8,128)(2,1)} copy(bf16[16,128,1536]{2,1,0:T(8,128)(2,1)S(1)} %bitcast.54) | data formatting | bytes 12582912 | tf_op jit(solution)/shard_map/reshape | solution.py:25
  26.8 6.7 %all-to-all-start = ((bf16[16,128,1536]{2,0,1:T(8,128)(2,1)}), bf16[16,128,1536]{2,0,1:T(8,128)(2,1)}, u32[]{:S(2)}, u32[]{:S(2)}) async-start(bf16[16,128,1536]{2,0,1:T(8,128)(2,1)} %copy.19), calls=%async_computation | async-start | bytes 12582912 | tf_op jit(solution)/shard_map/all_to_all | solution.py:35
  33.5 0.7 fusion.4
  39.2 0.7 fusion.5
  55.2 1.5 constant_dynamic-slice_fusion
  57.0 127.9 %all_gather.3 = bf16[256,8,192]{2,1,0:T(8,128)(2,1)S(1)} all-gather(bf16[16,8,192]{2,1,0:T(8,128)(2,1)S(1)} %stack.3), channel_id=1, replica_groups=mesh['mol'=2,'occ'=16] {'occ'}, dimensions={0}, use_global_device_ids=true | all-gather | bytes 835584 | tf_op jit(solution)/shard_map/all_gather | solution.py:34
  184.8 1.0 copy.21
  185.9 6.9 %copy.20 = bf16[16,16,8,1536]{3,2,1,0:T(8,128)(2,1)S(1)} copy(bf16[16,16,8,1536]{3,1,2,0:T(8,128)(2,1)} %bitcast.10) | data formatting | bytes 12582912 | tf_op jit(solution)/shard_map/all_to_all | solution.py:35
  192.9 4.7 %copy.22 = bf16[256,8,1536]{2,0,1:T(8,128)(2,1)} copy(bf16[256,8,1536]{2,1,0:T(8,128)(2,1)S(1)} %bitcast.52) | data formatting | bytes 12582912 | tf_op jit(solution)/shard_map/while | solution.py:47
  197.6 87.4 %while.13 = (s32[]{:T(128)}, f32[8,8]{0,1:T(8,128)S(1)}, bf16[256,8,192]{0,2,1:T(8,128)(2,1)S(1)}, bf16[256,8,1536]{2,0,1:T(8,128)(2,1)}, f32[1536]{0:T(1024)S(1...) while((s32[]{:T(128)}, f32[8,8]{0,1:T(8,128)S(1)}, ...), condition=%wide.region_2.3_spmd, body=%wide.region_0.2_spmd.sunk | while | flops 1220050944 | bytes 8758441 | solution.py:47
  199.1 0.6 dynamic_slice.90
  202.2 6.3 %fusion.14 = f32[8]{0:T(128)S(1)} fusion(bf16[256,8,1536]{2,0,1:T(8,128)(2,1)} %get-tuple-element.307, f32[]{:T(128)} %bitcast.50, f32[8]{0:T(128)S(1)} %get-tuple-element.310, f32[1536,192]{0,1:T(8,128)S(1)} %broadcast_add_fusion.2, bf16[256,8,192]{0,2,1:T(8,128)(2,1)S(1)} %get-tuple-element.306, s32[]{:T(128)} %get-tuple-element.290), kind=kOutput, calls=%fused_computation.1.clone.1 | convolution fusion | flops 1219756032 | bytes 7569960 | tf_op jit(solution)/shard_map/while/body/eval_jaxpr/dot_general | solution.py:10
  210.0 0.6 dynamic_slice.90
  213.1 6.3 %fusion.14 = f32[8]{0:T(128)S(1)} fusion(bf16[256,8,1536]{2,0,1:T(8,128)(2,1)} %get-tuple-element.307, f32[]{:T(128)} %bitcast.50, f32[8]{0:T(128)S(1)} %get-tuple-element.310, f32[1536,192]{0,1:T(8,128)S(1)} %broadcast_add_fusion.2, bf16[256,8,192]{0,2,1:T(8,128)(2,1)S(1)} %get-tuple-element.306, s32[]{:T(128)} %get-tuple-element.290), kind=kOutput, calls=%fused_computation.1.clone.1 | convolution fusion | flops 1219756032 | bytes 7569960 | tf_op jit(solution)/shard_map/while/body/eval_jaxpr/dot_general | solution.py:10
  224.1 6.3 %fusion.14 = f32[8]{0:T(128)S(1)} fusion(bf16[256,8,1536]{2,0,1:T(8,128)(2,1)} %get-tuple-element.307, f32[]{:T(128)} %bitcast.50, f32[8]{0:T(128)S(1)} %get-tuple-element.310, f32[1536,192]{0,1:T(8,128)S(1)} %broadcast_add_fusion.2, bf16[256,8,192]{0,2,1:T(8,128)(2,1)S(1)} %get-tuple-element.306, s32[]{:T(128)} %get-tuple-element.290), kind=kOutput, calls=%fused_computation.1.clone.1 | convolution fusion | flops 1219756032 | bytes 7569960 | tf_op jit(solution)/shard_map/while/body/eval_jaxpr/dot_general | solution.py:10
  235.0 6.3 %fusion.14 = f32[8]{0:T(128)S(1)} fusion(bf16[256,8,1536]{2,0,1:T(8,128)(2,1)} %get-tuple-element.307, f32[]{:T(128)} %bitcast.50, f32[8]{0:T(128)S(1)} %get-tuple-element.310, f32[1536,192]{0,1:T(8,128)S(1)} %broadcast_add_fusion.2, bf16[256,8,192]{0,2,1:T(8,128)(2,1)S(1)} %get-tuple-element.306, s32[]{:T(128)} %get-tuple-element.290), kind=kOutput, calls=%fused_computation.1.clone.1 | convolution fusion | flops 1219756032 | bytes 7569960 | tf_op jit(solution)/shard_map/while/body/eval_jaxpr/dot_general | solution.py:10
  245.9 6.3 %fusion.14 = f32[8]{0:T(128)S(1)} fusion(bf16[256,8,1536]{2,0,1:T(8,128)(2,1)} %get-tuple-element.307, f32[]{:T(128)} %bitcast.50, f32[8]{0:T(128)S(1)} %get-tuple-element.310, f32[1536,192]{0,1:T(8,128)S(1)} %broadcast_add_fusion.2, bf16[256,8,192]{0,2,1:T(8,128)(2,1)S(1)} %get-tuple-element.306, s32[]{:T(128)} %get-tuple-element.290), kind=kOutput, calls=%fused_computation.1.clone.1 | convolution fusion | flops 1219756032 | bytes 7569960 | tf_op jit(solution)/shard_map/while/body/eval_jaxpr/dot_general | solution.py:10
  256.9 6.3 %fusion.14 = f32[8]{0:T(128)S(1)} fusion(bf16[256,8,1536]{2,0,1:T(8,128)(2,1)} %get-tuple-element.307, f32[]{:T(128)} %bitcast.50, f32[8]{0:T(128)S(1)} %get-tuple-element.310, f32[1536,192]{0,1:T(8,128)S(1)} %broadcast_add_fusion.2, bf16[256,8,192]{0,2,1:T(8,128)(2,1)S(1)} %get-tuple-element.306, s32[]{:T(128)} %get-tuple-element.290), kind=kOutput, calls=%fused_computation.1.clone.1 | convolution fusion | flops 1219756032 | bytes 7569960 | tf_op jit(solution)/shard_map/while/body/eval_jaxpr/dot_general | solution.py:10
  264.7 0.6 dynamic_slice.90
  267.8 6.3 %fusion.14 = f32[8]{0:T(128)S(1)} fusion(bf16[256,8,1536]{2,0,1:T(8,128)(2,1)} %get-tuple-element.307, f32[]{:T(128)} %bitcast.50, f32[8]{0:T(128)S(1)} %get-tuple-element.310, f32[1536,192]{0,1:T(8,128)S(1)} %broadcast_add_fusion.2, bf16[256,8,192]{0,2,1:T(8,128)(2,1)S(1)} %get-tuple-element.306, s32[]{:T(128)} %get-tuple-element.290), kind=kOutput, calls=%fused_computation.1.clone.1 | convolution fusion | flops 1219756032 | bytes 7569960 | tf_op jit(solution)/shard_map/while/body/eval_jaxpr/dot_general | solution.py:10
  278.7 6.3 %fusion.14 = f32[8]{0:T(128)S(1)} fusion(bf16[256,8,1536]{2,0,1:T(8,128)(2,1)} %get-tuple-element.307, f32[]{:T(128)} %bitcast.50, f32[8]{0:T(128)S(1)} %get-tuple-element.310, f32[1536,192]{0,1:T(8,128)S(1)} %broadcast_add_fusion.2, bf16[256,8,192]{0,2,1:T(8,128)(2,1)S(1)} %get-tuple-element.306, s32[]{:T(128)} %get-tuple-element.290), kind=kOutput, calls=%fused_computation.1.clone.1 | convolution fusion | flops 1219756032 | bytes 7569960 | tf_op jit(solution)/shard_map/while/body/eval_jaxpr/dot_general | solution.py:10
  285.0 0.7 copy.23
  (68 shorter events, 15.2 us)
Async XLA Ops:
  17.9 2.6 copy-start.1
  26.7 6.8 %copy-start.4 = (s32[8]{0:T(128)S(1)}, s32[8]{0:T(128)}, u32[]{:S(2)}) copy-start(s32[8]{0:T(128)} %param.13) | copy-start | bytes 100
  26.7 12.5 %copy-start.3 = (s32[8]{0:T(128)S(1)}, s32[8]{0:T(128)}, u32[]{:S(2)}) copy-start(s32[8]{0:T(128)} %param.12) | copy-start | bytes 100
  26.7 159.1 %copy-start.5 = (f32[128]{0:T(128)S(1)}, f32[128]{0:T(128)}, u32[]{:S(2)}) copy-start(f32[128]{0:T(128)} %param.10) | copy-start | bytes 1540
  26.8 159.2 %all-to-all-start = ((bf16[16,128,1536]{2,0,1:T(8,128)(2,1)}), bf16[16,128,1536]{2,0,1:T(8,128)(2,1)}, u32[]{:S(2)}, u32[]{:S(2)}) async-start(bf16[16,128,1536]{2,0,1:T(8,128)(2,1)} %copy.19), calls=%async_computation | async-start | bytes 12582912 | tf_op jit(solution)/shard_map/all_to_all | solution.py:35
  192.8 4.7 %copy-start = (bf16[16,16,8,1536]{3,2,1,0:T(8,128)(2,1)}, bf16[16,16,8,1536]{3,2,1,0:T(8,128)(2,1)S(1)}, u32[]{:S(2)}) copy-start(bf16[16,16,8,1536]{3,2,1,0:T(8,128)(2,1)S(1)} %copy.20) | copy-start | bytes 18874372
  192.8 4.7 %copy-start.2 = (f32[1536]{0:T(1024)S(1)}, f32[1536]{0:T(1024)}, u32[]{:S(2)}) copy-start(f32[1536]{0:T(1024)} %param.11) | copy-start | bytes 18436
where the time goes:
time: 287 us; the launch traced here: 286 us
  blocking collectives  128 us (45%)
  matrix products  67.4 us (23%)
  local copies, waits for them, and re-layouts  40.8 us (14%)
  between operations  21.1 us (7%)
  loops' own time  20.6 us (7%)
  starting transfers between devices  6.74 us (2%)
    all_gather x1, blocking collectives, per_device(): blocks = lax.all_gather(pieces, 'occ', axis=0, tiled=True)  128 us
    dot_general x8, matrix products, pair_column(): lax.dot_general(factors, block, (((0,), (0,)), ((), ())), preferred_eleme...  50.1 us
    another operation x1, loops' own time, per_device(): energies = lax.fori_loop(0, step_count, step_body, energies)  20.6 us
    dot_general x1, matrix products, per_device(): jnp.dot(flat, orbitals, preferred_element_type=jnp.float32)  17.3 us
    all_to_all x1, local copies, waits for them, and re-layouts, per_device(): lax.all_to_all(product, 'occ', split_axis=1, concat_axis=0, tiled=True)  6.9 us
    all_to_all x1, starting transfers between devices, per_device(): lax.all_to_all(product, 'occ', split_axis=1, concat_axis=0, tiled=True)  6.74 us
    reshape x1, local copies, waits for them, and re-layouts, per_device(): product = product.reshape(aux_here, occ_total, orbitals.shape[1])  6.2 us
  transfers between devices with their start and end apart: 1, of which 0 were waited for; matrix products, arithmetic and copies ran while one was open for 1% of the time, Pallas kernels for 0%

commit v1 on v0

--- a/solution.py
+++ b/solution.py
@@ -1,9 +1,29 @@
+import functools
 import jax
 import jax.numpy as jnp
 from jax import lax
 from jax.sharding import PartitionSpec as P
 
 VBLK = 192
+
+
+def view_arrays(s0, link_axis, d0):
+    dev_n = jax.lax.axis_size(link_axis)
+    pieces_in = [(it, (it + 1) % dev_n) for it in range(dev_n)]
+    fields = [(it, (it - 1) % dev_n) for it in range(dev_n)]
+    part_next, h_now = ([s0], [s0])
+    for _ in range(dev_n // 2):
+        part_next.append(jax.lax.ppermute(part_next[-1], axis_name=link_axis, perm=pieces_in))
+    for _ in range((dev_n - 1) // 2):
+        h_now.append(jax.lax.ppermute(h_now[-1], axis_name=link_axis, perm=fields))
+    return jnp.roll(
+        jnp.concatenate([*part_next[::-1], *h_now[1:]], axis=d0),
+        (jax.lax.axis_index(link_axis) - dev_n // 2) * s0.shape[d0],
+        axis=d0,
+    )
+
+
+replace_the_skins = functools.partial(view_arrays, link_axis="occ", d0=0)
 
 
 def pair_column(factors, block, occ_here, occ_energy, vir_energy, orbital_j, block_id):
@@ -31,7 +51,7 @@
         return piece[:, 0, :]
 
     pieces = jnp.stack([own_piece(step) for step in range(step_count)], axis=1)
-    blocks = lax.all_gather(pieces, "occ", axis=0, tiled=True)
+    blocks = replace_the_skins(pieces)
     factors = lax.all_to_all(product, "occ", split_axis=1, concat_axis=0, tiled=True)
     local_count = factors.shape[1]
     occ_here = lax.dynamic_slice(occ_energy, (lax.axis_index("occ") * local_count,), (local_count,))

time: 287 us -> 308 us (1.073); the launches traced: 286 us -> 302 us
  starting transfers between devices: 6.74 us -> 136 us
  blocking collectives: 128 us -> 0 us
  waiting for transfers between devices: 0.01 us -> 15 us
    ppermute x0 -> x15, starting transfers between devices: none -> 129 us  [the longest x7 76.9 us: view_arrays(): h_now.append(jax.lax.ppermute(h_now[-1], axis_name=link_axis, perm=fields))]
    all_gather x1 -> x0, blocking collectives: 128 us -> none  [per_device(): blocks = lax.all_gather(pieces, 'occ', axis=0, tiled=True)]
    ppermute x0 -> x15, waiting for transfers between devices: none -> 15 us  [the longest x7 10.6 us: view_arrays(): h_now.append(jax.lax.ppermute(h_now[-1], axis_name=link_axis, perm=fields))]
  transfers between devices with their start and end apart: 1 -> 16, of which waited for: 0 -> 15; matrix products, arithmetic and copies ran while one was open for 1% -> 1% of each run, Pallas kernels for 0% -> 0%
where the time goes in v1:
time: 308 us; the launch traced here: 302 us
  starting transfers between devices  136 us (44%)
  matrix products  67.4 us (22%)
  local copies, waits for them, and re-layouts  41 us (13%)
  between operations  21 us (7%)
  loops' own time  20.6 us (7%)
  waiting for transfers between devices  15 us (5%)
    ppermute x7, starting transfers between devices, view_arrays(): h_now.append(jax.lax.ppermute(h_now[-1], axis_name=link_axis, perm=fields))  76.9 us
    ppermute x8, starting transfers between devices, view_arrays(): jax.lax.ppermute(part_next[-1], axis_name=link_axis, perm=pieces_in)  52.4 us
    dot_general x8, matrix products, pair_column(): lax.dot_general(factors, block, (((0,), (0,)), ((), ())), preferred_eleme...  50.1 us
    another operation x1, loops' own time, per_device(): energies = lax.fori_loop(0, step_count, step_body, energies)  20.6 us
    dot_general x1, matrix products, per_device(): jnp.dot(flat, orbitals, preferred_element_type=jnp.float32)  17.3 us
    ppermute x7, waiting for transfers between devices, view_arrays(): h_now.append(jax.lax.ppermute(h_now[-1], axis_name=link_axis, perm=fields))  10.6 us
    all_to_all x1, local copies, waits for them, and re-layouts, per_device(): lax.all_to_all(product, 'occ', split_axis=1, concat_axis=0, tiled=True)  6.9 us
    all_to_all x1, starting transfers between devices, per_device(): lax.all_to_all(product, 'occ', split_axis=1, concat_axis=0, tiled=True)  6.74 us
  transfers between devices with their start and end apart: 16, of which 15 were waited for; matrix products, arithmetic and copies ran while one was open for 1% of the time, Pallas kernels for 0%

profile of v1, /device:TPU:9, one launch (start us, length us, event | category | flops | bytes accessed | tf_op | source)
XLA Modules:
  0.0 302.3 jit_solution(3350813820761481469)
XLA Ops:
  0.6 17.3 %convolution_convert_fusion = bf16[2048,1536]{1,0:T(8,128)(2,1)S(1)} fusion(bf16[2048,2048]{1,0:T(8,128)(2,1)} %bitcast.56, bf16[2048,1536]{1,0:T(8,128)(2,1)} %param.9), kind=kOutput, calls=%fused_computation.7 | convolution fusion | flops 12888047616 | bytes 20971520 | tf_op jit(solution)/shard_map/dot_general | solution.py:44
  17.9 2.6 copy-done.1
  20.5 6.2 %copy.19 = bf16[16,128,1536]{2,0,1:T(8,128)(2,1)} copy(bf16[16,128,1536]{2,1,0:T(8,128)(2,1)S(1)} %bitcast.54) | data formatting | bytes 12582912 | tf_op jit(solution)/shard_map/reshape | solution.py:45
  26.7 6.7 %all-to-all-start = ((bf16[16,128,1536]{2,0,1:T(8,128)(2,1)}), bf16[16,128,1536]{2,0,1:T(8,128)(2,1)}, u32[]{:S(2)}, u32[]{:S(2)}) async-start(bf16[16,128,1536]{2,0,1:T(8,128)(2,1)} %copy.19), calls=%async_computation | async-start | bytes 12582912 | tf_op jit(solution)/shard_map/all_to_all | solution.py:55
  60.2 2.5 collective-permute-start.1
  62.6 76.9 %collective-permute-start.8 = (bf16[16,8,192]{2,1,0:T(8,128)(2,1)S(1)}, bf16[16,8,192]{2,1,0:T(8,128)(2,1)S(1)}, u32[]{:S(2)}, u32[]{:S(2)}) collective-permute-start(bf16[16,8,192]{2,1,0:T(8,128)(2,1)S(1)} %stack.3), channel_id=1, source_target_pairs={{0,15},{1,0},{2,1},{3,2},{4,3},{5,4},{6,5},{7,6},{8,7},{9,8},{10,9... | collective-permute-start | bytes 147464 | tf_op jit(solution)/shard_map/ppermute | solution.py:18
  140.2 32.0 %collective-permute-start.2 = (bf16[16,8,192]{2,1,0:T(8,128)(2,1)S(1)}, bf16[16,8,192]{2,1,0:T(8,128)(2,1)S(1)}, u32[]{:S(2)}, u32[]{:S(2)}) collective-permute-start(bf16[16,8,192]{2,1,0:T(8,128)(2,1)S(1)} %collective-permute-done.1), channel_id=1, source_target_pairs={{0,1},{1,2},{2,3},{3,4},{4,5},{5,6},{6,7},{7,8},{8,9},{9,10},{10,1... | collective-permute-start | bytes 147464 | tf_op jit(solution)/shard_map/ppermute | solution.py:16
  173.6 3.4 %collective-permute-start.3 = (bf16[16,8,192]{2,1,0:T(8,128)(2,1)S(1)}, bf16[16,8,192]{2,1,0:T(8,128)(2,1)S(1)}, u32[]{:S(2)}, u32[]{:S(2)}) collective-permute-start(bf16[16,8,192]{2,1,0:T(8,128)(2,1)S(1)} %collective-permute-done.2), channel_id=1, source_target_pairs={{0,1},{1,2},{2,3},{3,4},{4,5},{5,6},{6,7},{7,8},{8,9},{9,10},{10,1... | collective-permute-start | bytes 147464 | tf_op jit(solution)/shard_map/ppermute | solution.py:16
  178.3 3.3 %collective-permute-start.4 = (bf16[16,8,192]{2,1,0:T(8,128)(2,1)S(1)}, bf16[16,8,192]{2,1,0:T(8,128)(2,1)S(1)}, u32[]{:S(2)}, u32[]{:S(2)}) collective-permute-start(bf16[16,8,192]{2,1,0:T(8,128)(2,1)S(1)} %collective-permute-done.3), channel_id=1, source_target_pairs={{0,1},{1,2},{2,3},{3,4},{4,5},{5,6},{6,7},{7,8},{8,9},{9,10},{10,1... | collective-permute-start | bytes 147464 | tf_op jit(solution)/shard_map/ppermute | solution.py:16
  182.9 3.3 %collective-permute-start.5 = (bf16[16,8,192]{2,1,0:T(8,128)(2,1)S(1)}, bf16[16,8,192]{2,1,0:T(8,128)(2,1)S(1)}, u32[]{:S(2)}, u32[]{:S(2)}) collective-permute-start(bf16[16,8,192]{2,1,0:T(8,128)(2,1)S(1)} %collective-permute-done.4), channel_id=1, source_target_pairs={{0,1},{1,2},{2,3},{3,4},{4,5},{5,6},{6,7},{7,8},{8,9},{9,10},{10,1... | collective-permute-start | bytes 147464 | tf_op jit(solution)/shard_map/ppermute | solution.py:16
  187.5 3.3 %collective-permute-start.6 = (bf16[16,8,192]{2,1,0:T(8,128)(2,1)S(1)}, bf16[16,8,192]{2,1,0:T(8,128)(2,1)S(1)}, u32[]{:S(2)}, u32[]{:S(2)}) collective-permute-start(bf16[16,8,192]{2,1,0:T(8,128)(2,1)S(1)} %collective-permute-done.5), channel_id=1, source_target_pairs={{0,1},{1,2},{2,3},{3,4},{4,5},{5,6},{6,7},{7,8},{8,9},{9,10},{10,1... | collective-permute-start | bytes 147464 | tf_op jit(solution)/shard_map/ppermute | solution.py:16
  192.0 3.3 %collective-permute-start.7 = (bf16[16,8,192]{2,1,0:T(8,128)(2,1)S(1)}, bf16[16,8,192]{2,1,0:T(8,128)(2,1)S(1)}, u32[]{:S(2)}, u32[]{:S(2)}) collective-permute-start(bf16[16,8,192]{2,1,0:T(8,128)(2,1)S(1)} %collective-permute-done.6), channel_id=1, source_target_pairs={{0,1},{1,2},{2,3},{3,4},{4,5},{5,6},{6,7},{7,8},{8,9},{9,10},{10,1... | collective-permute-start | bytes 147464 | tf_op jit(solution)/shard_map/ppermute | solution.py:16
  196.8 4.4 %collective-permute-done.14 = bf16[16,8,192]{2,1,0:T(8,128)(2,1)S(1)} collective-permute-done((bf16[16,8,192]{2,1,0:T(8,128)(2,1)S(1)}, bf16[16,8,192]{2,1,0:T(8,128)(2,1)S(1)}, u32[]{:S(2)}, u32[]{:S(2)}) %collective-permute-start.14) | collective-permute-done | bytes 49184 | tf_op jit(solution)/shard_map/ppermute | solution.py:18
  202.5 6.9 %copy.20 = bf16[16,16,8,1536]{3,2,1,0:T(8,128)(2,1)S(1)} copy(bf16[16,16,8,1536]{3,1,2,0:T(8,128)(2,1)} %bitcast.10) | data formatting | bytes 12582912 | tf_op jit(solution)/shard_map/all_to_all | solution.py:55
  209.5 4.7 %copy.22 = bf16[256,8,1536]{2,0,1:T(8,128)(2,1)} copy(bf16[256,8,1536]{2,1,0:T(8,128)(2,1)S(1)} %bitcast.52) | data formatting | bytes 12582912 | tf_op jit(solution)/shard_map/while | solution.py:67
  214.2 87.4 %while.13 = (s32[]{:T(128)}, f32[8,8]{0,1:T(8,128)S(1)}, bf16[256,8,192]{0,2,1:T(8,128)(2,1)S(1)}, bf16[256,8,1536]{2,0,1:T(8,128)(2,1)}, f32[1536]{0:T(1024)S(1...) while((s32[]{:T(128)}, f32[8,8]{0,1:T(8,128)S(1)}, ...), condition=%wide.region_2.3_spmd, body=%wide.region_0.2_spmd.sunk | while | flops 1220050944 | bytes 8758441 | solution.py:67
  218.8 6.3 %fusion.14 = f32[8]{0:T(128)S(1)} fusion(bf16[256,8,1536]{2,0,1:T(8,128)(2,1)} %get-tuple-element.307, f32[]{:T(128)} %bitcast.50, f32[8]{0:T(128)S(1)} %get-tuple-element.310, f32[1536,192]{0,1:T(8,128)S(1)} %broadcast_add_fusion.2, bf16[256,8,192]{0,2,1:T(8,128)(2,1)S(1)} %get-tuple-element.306, s32[]{:T(128)} %get-tuple-element.290), kind=kOutput, calls=%fused_computation.1.clone.1 | convolution fusion | flops 1219756032 | bytes 7569960 | tf_op jit(solution)/shard_map/while/body/eval_jaxpr/dot_general | solution.py:30
  229.7 6.3 %fusion.14 = f32[8]{0:T(128)S(1)} fusion(bf16[256,8,1536]{2,0,1:T(8,128)(2,1)} %get-tuple-element.307, f32[]{:T(128)} %bitcast.50, f32[8]{0:T(128)S(1)} %get-tuple-element.310, f32[1536,192]{0,1:T(8,128)S(1)} %broadcast_add_fusion.2, bf16[256,8,192]{0,2,1:T(8,128)(2,1)S(1)} %get-tuple-element.306, s32[]{:T(128)} %get-tuple-element.290), kind=kOutput, calls=%fused_computation.1.clone.1 | convolution fusion | flops 1219756032 | bytes 7569960 | tf_op jit(solution)/shard_map/while/body/eval_jaxpr/dot_general | solution.py:30
  240.7 6.3 %fusion.14 = f32[8]{0:T(128)S(1)} fusion(bf16[256,8,1536]{2,0,1:T(8,128)(2,1)} %get-tuple-element.307, f32[]{:T(128)} %bitcast.50, f32[8]{0:T(128)S(1)} %get-tuple-element.310, f32[1536,192]{0,1:T(8,128)S(1)} %broadcast_add_fusion.2, bf16[256,8,192]{0,2,1:T(8,128)(2,1)S(1)} %get-tuple-element.306, s32[]{:T(128)} %get-tuple-element.290), kind=kOutput, calls=%fused_computation.1.clone.1 | convolution fusion | flops 1219756032 | bytes 7569960 | tf_op jit(solution)/shard_map/while/body/eval_jaxpr/dot_general | solution.py:30
  251.6 6.3 %fusion.14 = f32[8]{0:T(128)S(1)} fusion(bf16[256,8,1536]{2,0,1:T(8,128)(2,1)} %get-tuple-element.307, f32[]{:T(128)} %bitcast.50, f32[8]{0:T(128)S(1)} %get-tuple-element.310, f32[1536,192]{0,1:T(8,128)S(1)} %broadcast_add_fusion.2, bf16[256,8,192]{0,2,1:T(8,128)(2,1)S(1)} %get-tuple-element.306, s32[]{:T(128)} %get-tuple-element.290), kind=kOutput, calls=%fused_computation.1.clone.1 | convolution fusion | flops 1219756032 | bytes 7569960 | tf_op jit(solution)/shard_map/while/body/eval_jaxpr/dot_general | solution.py:30
  262.5 6.3 %fusion.14 = f32[8]{0:T(128)S(1)} fusion(bf16[256,8,1536]{2,0,1:T(8,128)(2,1)} %get-tuple-element.307, f32[]{:T(128)} %bitcast.50, f32[8]{0:T(128)S(1)} %get-tuple-element.310, f32[1536,192]{0,1:T(8,128)S(1)} %broadcast_add_fusion.2, bf16[256,8,192]{0,2,1:T(8,128)(2,1)S(1)} %get-tuple-element.306, s32[]{:T(128)} %get-tuple-element.290), kind=kOutput, calls=%fused_computation.1.clone.1 | convolution fusion | flops 1219756032 | bytes 7569960 | tf_op jit(solution)/shard_map/while/body/eval_jaxpr/dot_general | solution.py:30
  273.5 6.3 %fusion.14 = f32[8]{0:T(128)S(1)} fusion(bf16[256,8,1536]{2,0,1:T(8,128)(2,1)} %get-tuple-element.307, f32[]{:T(128)} %bitcast.50, f32[8]{0:T(128)S(1)} %get-tuple-element.310, f32[1536,192]{0,1:T(8,128)S(1)} %broadcast_add_fusion.2, bf16[256,8,192]{0,2,1:T(8,128)(2,1)S(1)} %get-tuple-element.306, s32[]{:T(128)} %get-tuple-element.290), kind=kOutput, calls=%fused_computation.1.clone.1 | convolution fusion | flops 1219756032 | bytes 7569960 | tf_op jit(solution)/shard_map/while/body/eval_jaxpr/dot_general | solution.py:30
  284.4 6.3 %fusion.14 = f32[8]{0:T(128)S(1)} fusion(bf16[256,8,1536]{2,0,1:T(8,128)(2,1)} %get-tuple-element.307, f32[]{:T(128)} %bitcast.50, f32[8]{0:T(128)S(1)} %get-tuple-element.310, f32[1536,192]{0,1:T(8,128)S(1)} %broadcast_add_fusion.2, bf16[256,8,192]{0,2,1:T(8,128)(2,1)S(1)} %get-tuple-element.306, s32[]{:T(128)} %get-tuple-element.290), kind=kOutput, calls=%fused_computation.1.clone.1 | convolution fusion | flops 1219756032 | bytes 7569960 | tf_op jit(solution)/shard_map/while/body/eval_jaxpr/dot_general | solution.py:30
  295.3 6.3 %fusion.14 = f32[8]{0:T(128)S(1)} fusion(bf16[256,8,1536]{2,0,1:T(8,128)(2,1)} %get-tuple-element.307, f32[]{:T(128)} %bitcast.50, f32[8]{0:T(128)S(1)} %get-tuple-element.310, f32[1536,192]{0,1:T(8,128)S(1)} %broadcast_add_fusion.2, bf16[256,8,192]{0,2,1:T(8,128)(2,1)S(1)} %get-tuple-element.306, s32[]{:T(128)} %get-tuple-element.290), kind=kOutput, calls=%fused_computation.1.clone.1 | convolution fusion | flops 1219756032 | bytes 7569960 | tf_op jit(solution)/shard_map/while/body/eval_jaxpr/dot_general | solution.py:30
  (130 shorter events, 34.0 us)
Async XLA Ops:
  17.9 2.6 copy-start.1
  26.7 6.8 %copy-start.4 = (s32[8]{0:T(128)S(1)}, s32[8]{0:T(128)}, u32[]{:S(2)}) copy-start(s32[8]{0:T(128)} %param.13) | copy-start | bytes 100
  26.7 12.3 %copy-start.3 = (s32[8]{0:T(128)S(1)}, s32[8]{0:T(128)}, u32[]{:S(2)}) copy-start(s32[8]{0:T(128)} %param.12) | copy-start | bytes 100
  26.7 168.6 %copy-start.5 = (f32[128]{0:T(128)S(1)}, f32[128]{0:T(128)}, u32[]{:S(2)}) copy-start(f32[128]{0:T(128)} %param.10) | copy-start | bytes 1540
  26.7 175.8 %all-to-all-start = ((bf16[16,128,1536]{2,0,1:T(8,128)(2,1)}), bf16[16,128,1536]{2,0,1:T(8,128)(2,1)}, u32[]{:S(2)}, u32[]{:S(2)}) async-start(bf16[16,128,1536]{2,0,1:T(8,128)(2,1)} %copy.19), calls=%async_computation | async-start | bytes 12582912 | tf_op jit(solution)/shard_map/all_to_all | solution.py:55
  56.6 3.5 %collective-permute-start = (bf16[16,8,192]{2,1,0:T(8,128)(2,1)S(1)}, bf16[16,8,192]{2,1,0:T(8,128)(2,1)S(1)}, u32[]{:S(2)}, u32[]{:S(2)}) collective-permute-start(bf16[16,8,192]{2,1,0:T(8,128)(2,1)S(1)} %stack.3), channel_id=1, source_target_pairs={{0,1},{1,2},{2,3},{3,4},{4,5},{5,6},{6,7},{7,8},{8,9},{9,10},{10,1... | collective-permute-start | bytes 147464 | tf_op jit(solution)/shard_map/ppermute | solution.py:16
  60.2 80.1 %collective-permute-start.1 = (bf16[16,8,192]{2,1,0:T(8,128)(2,1)S(1)}, bf16[16,8,192]{2,1,0:T(8,128)(2,1)S(1)}, u32[]{:S(2)}, u32[]{:S(2)}) collective-permute-start(bf16[16,8,192]{2,1,0:T(8,128)(2,1)S(1)} %collective-permute-done), channel_id=1, source_target_pairs={{0,1},{1,2},{2,3},{3,4},{4,5},{5,6},{6,7},{7,8},{8,9},{9,10},{10,1... | collective-permute-start | bytes 147464 | tf_op jit(solution)/shard_map/ppermute | solution.py:16
  62.6 110.6 %collective-permute-start.8 = (bf16[16,8,192]{2,1,0:T(8,128)(2,1)S(1)}, bf16[16,8,192]{2,1,0:T(8,128)(2,1)S(1)}, u32[]{:S(2)}, u32[]{:S(2)}) collective-permute-start(bf16[16,8,192]{2,1,0:T(8,128)(2,1)S(1)} %stack.3), channel_id=1, source_target_pairs={{0,15},{1,0},{2,1},{3,2},{4,3},{5,4},{6,5},{7,6},{8,7},{9,8},{10,9... | collective-permute-start | bytes 147464 | tf_op jit(solution)/shard_map/ppermute | solution.py:18
  140.2 33.3 %collective-permute-start.2 = (bf16[16,8,192]{2,1,0:T(8,128)(2,1)S(1)}, bf16[16,8,192]{2,1,0:T(8,128)(2,1)S(1)}, u32[]{:S(2)}, u32[]{:S(2)}) collective-permute-start(bf16[16,8,192]{2,1,0:T(8,128)(2,1)S(1)} %collective-permute-done.1), channel_id=1, source_target_pairs={{0,1},{1,2},{2,3},{3,4},{4,5},{5,6},{6,7},{7,8},{8,9},{9,10},{10,1... | collective-permute-start | bytes 147464 | tf_op jit(solution)/shard_map/ppermute | solution.py:16
  173.3 4.7 %collective-permute-start.9 = (bf16[16,8,192]{2,1,0:T(8,128)(2,1)S(1)}, bf16[16,8,192]{2,1,0:T(8,128)(2,1)S(1)}, u32[]{:S(2)}, u32[]{:S(2)}) collective-permute-start(bf16[16,8,192]{2,1,0:T(8,128)(2,1)S(1)} %collective-permute-done.8), channel_id=1, source_target_pairs={{0,15},{1,0},{2,1},{3,2},{4,3},{5,4},{6,5},{7,6},{8,7},{9,8},{10,9... | collective-permute-start | bytes 147464 | tf_op jit(solution)/shard_map/ppermute | solution.py:18
  173.6 4.7 %collective-permute-start.3 = (bf16[16,8,192]{2,1,0:T(8,128)(2,1)S(1)}, bf16[16,8,192]{2,1,0:T(8,128)(2,1)S(1)}, u32[]{:S(2)}, u32[]{:S(2)}) collective-permute-start(bf16[16,8,192]{2,1,0:T(8,128)(2,1)S(1)} %collective-permute-done.2), channel_id=1, source_target_pairs={{0,1},{1,2},{2,3},{3,4},{4,5},{5,6},{6,7},{7,8},{8,9},{9,10},{10,1... | collective-permute-start | bytes 147464 | tf_op jit(solution)/shard_map/ppermute | solution.py:16
  178.0 4.6 %collective-permute-start.10 = (bf16[16,8,192]{2,1,0:T(8,128)(2,1)S(1)}, bf16[16,8,192]{2,1,0:T(8,128)(2,1)S(1)}, u32[]{:S(2)}, u32[]{:S(2)}) collective-permute-start(bf16[16,8,192]{2,1,0:T(8,128)(2,1)S(1)} %collective-permute-done.9), channel_id=1, source_target_pairs={{0,15},{1,0},{2,1},{3,2},{4,3},{5,4},{6,5},{7,6},{8,7},{9,8},{10,9... | collective-permute-start | bytes 147464 | tf_op jit(solution)/shard_map/ppermute | solution.py:18
  178.3 4.6 %collective-permute-start.4 = (bf16[16,8,192]{2,1,0:T(8,128)(2,1)S(1)}, bf16[16,8,192]{2,1,0:T(8,128)(2,1)S(1)}, u32[]{:S(2)}, u32[]{:S(2)}) collective-permute-start(bf16[16,8,192]{2,1,0:T(8,128)(2,1)S(1)} %collective-permute-done.3), channel_id=1, source_target_pairs={{0,1},{1,2},{2,3},{3,4},{4,5},{5,6},{6,7},{7,8},{8,9},{9,10},{10,1... | collective-permute-start | bytes 147464 | tf_op jit(solution)/shard_map/ppermute | solution.py:16
  182.6 4.6 %collective-permute-start.11 = (bf16[16,8,192]{2,1,0:T(8,128)(2,1)S(1)}, bf16[16,8,192]{2,1,0:T(8,128)(2,1)S(1)}, u32[]{:S(2)}, u32[]{:S(2)}) collective-permute-start(bf16[16,8,192]{2,1,0:T(8,128)(2,1)S(1)} %collective-permute-done.10), channel_id=1, source_target_pairs={{0,15},{1,0},{2,1},{3,2},{4,3},{5,4},{6,5},{7,6},{8,7},{9,8},{10,9... | collective-permute-start | bytes 147464 | tf_op jit(solution)/shard_map/ppermute | solution.py:18
  182.9 4.6 %collective-permute-start.5 = (bf16[16,8,192]{2,1,0:T(8,128)(2,1)S(1)}, bf16[16,8,192]{2,1,0:T(8,128)(2,1)S(1)}, u32[]{:S(2)}, u32[]{:S(2)}) collective-permute-start(bf16[16,8,192]{2,1,0:T(8,128)(2,1)S(1)} %collective-permute-done.4), channel_id=1, source_target_pairs={{0,1},{1,2},{2,3},{3,4},{4,5},{5,6},{6,7},{7,8},{8,9},{9,10},{10,1... | collective-permute-start | bytes 147464 | tf_op jit(solution)/shard_map/ppermute | solution.py:16
  187.2 4.6 %collective-permute-start.12 = (bf16[16,8,192]{2,1,0:T(8,128)(2,1)S(1)}, bf16[16,8,192]{2,1,0:T(8,128)(2,1)S(1)}, u32[]{:S(2)}, u32[]{:S(2)}) collective-permute-start(bf16[16,8,192]{2,1,0:T(8,128)(2,1)S(1)} %collective-permute-done.11), channel_id=1, source_target_pairs={{0,15},{1,0},{2,1},{3,2},{4,3},{5,4},{6,5},{7,6},{8,7},{9,8},{10,9... | collective-permute-start | bytes 147464 | tf_op jit(solution)/shard_map/ppermute | solution.py:18
  187.5 4.6 %collective-permute-start.6 = (bf16[16,8,192]{2,1,0:T(8,128)(2,1)S(1)}, bf16[16,8,192]{2,1,0:T(8,128)(2,1)S(1)}, u32[]{:S(2)}, u32[]{:S(2)}) collective-permute-start(bf16[16,8,192]{2,1,0:T(8,128)(2,1)S(1)} %collective-permute-done.5), channel_id=1, source_target_pairs={{0,1},{1,2},{2,3},{3,4},{4,5},{5,6},{6,7},{7,8},{8,9},{9,10},{10,1... | collective-permute-start | bytes 147464 | tf_op jit(solution)/shard_map/ppermute | solution.py:16
  191.8 4.6 %collective-permute-start.13 = (bf16[16,8,192]{2,1,0:T(8,128)(2,1)S(1)}, bf16[16,8,192]{2,1,0:T(8,128)(2,1)S(1)}, u32[]{:S(2)}, u32[]{:S(2)}) collective-permute-start(bf16[16,8,192]{2,1,0:T(8,128)(2,1)S(1)} %collective-permute-done.12), channel_id=1, source_target_pairs={{0,15},{1,0},{2,1},{3,2},{4,3},{5,4},{6,5},{7,6},{8,7},{9,8},{10,9... | collective-permute-start | bytes 147464 | tf_op jit(solution)/shard_map/ppermute | solution.py:18
  192.0 4.6 %collective-permute-start.7 = (bf16[16,8,192]{2,1,0:T(8,128)(2,1)S(1)}, bf16[16,8,192]{2,1,0:T(8,128)(2,1)S(1)}, u32[]{:S(2)}, u32[]{:S(2)}) collective-permute-start(bf16[16,8,192]{2,1,0:T(8,128)(2,1)S(1)} %collective-permute-done.6), channel_id=1, source_target_pairs={{0,1},{1,2},{2,3},{3,4},{4,5},{5,6},{6,7},{7,8},{8,9},{9,10},{10,1... | collective-permute-start | bytes 147464 | tf_op jit(solution)/shard_map/ppermute | solution.py:16
  196.4 4.8 %collective-permute-start.14 = (bf16[16,8,192]{2,1,0:T(8,128)(2,1)S(1)}, bf16[16,8,192]{2,1,0:T(8,128)(2,1)S(1)}, u32[]{:S(2)}, u32[]{:S(2)}) collective-permute-start(bf16[16,8,192]{2,1,0:T(8,128)(2,1)S(1)} %collective-permute-done.13), channel_id=1, source_target_pairs={{0,15},{1,0},{2,1},{3,2},{4,3},{5,4},{6,5},{7,6},{8,7},{9,8},{10,9... | collective-permute-start | bytes 147464 | tf_op jit(solution)/shard_map/ppermute | solution.py:18
  209.4 4.7 %copy-start = (bf16[16,16,8,1536]{3,2,1,0:T(8,128)(2,1)}, bf16[16,16,8,1536]{3,2,1,0:T(8,128)(2,1)S(1)}, u32[]{:S(2)}) copy-start(bf16[16,16,8,1536]{3,2,1,0:T(8,128)(2,1)S(1)} %copy.20) | copy-start | bytes 18874372
  209.5 4.7 %copy-start.2 = (f32[1536]{0:T(1024)S(1)}, f32[1536]{0:T(1024)}, u32[]{:S(2)}) copy-start(f32[1536]{0:T(1024)} %param.11) | copy-start | bytes 18436
